TPU v7x, 256 devices: a whole 4x4x8 slice. The times are simulated.
256 devices in a mesh: region: 8 (over z), rows: 32 (over y, x, core).
Axes of the slice: x: 4, y: 4, z: 8, core: 2. Of those that a mesh axis runs over, the one named last changes fastest.
Arguments:
- ensemble_state: float32 [524288, 256], P(('region', 'rows')), may hold values from -16 to 16
- obs_values: float32 [4, 1024], replicated, may hold values from -16 to 16
- obs_error: float32 [4, 1024], replicated, may hold values from 0.1 to 2
- batch_owner: int32 [4], replicated, may hold values from 0 to 7
- readers: int32 [4, 3], replicated, may hold values from 0 to 7
- obs_order: int32 [4, 1024], replicated, may hold values from 0 to 1023, each once within a row
- obs_rows: int32 [4, 1024], replicated, may hold values from 0 to 2047
- loc_taper: float32 [4, 8, 1024], replicated, may hold values from 0.02 to 0.3
Outputs:
- analysis: float32 [524288, 256], P(('region', 'rows'))
Inputs may be any that keep to these rules, and one draw needn't show every extreme that they name: Each row of obs_order holds every observation number once. `readers`: regions that read a batch besides its owner region; repeats allowed.
All inputs are finite; a program needn't handle non-finite values.
Results may differ from a plain program's by a relative error of at most 0.0024.
Values may be sent and summed in bfloat16 or wider, within the bound.
No kernel may reach another device: no remote copies, remote signals or barrier semaphores. Data moves between devices by JAX's collectives and lax.ppermute only.
A program may use at most 64 MiB of HBM per device.

v0:
```python
import jax
import jax.numpy as jnp
from jax import lax
from jax.experimental import pallas as pl
from jax.sharding import PartitionSpec as P


def adjust(prior_ens, values, errors):
    members = prior_ens.shape[1]
    prior_mean = jnp.mean(prior_ens, axis=1, keepdims=True)
    anomalies = prior_ens - prior_mean
    variance = jnp.sum(anomalies * anomalies, axis=1, keepdims=True) / (members - 1) + 1e-05
    errors = errors[:, None]
    values = values[:, None]
    post_var = variance * errors / (variance + errors)
    mean_shift = post_var * (prior_mean / variance + values / errors) - prior_mean
    shrink = jnp.sqrt(errors / (variance + errors))
    obs_incr = (mean_shift + (shrink - 1.0) * anomalies).astype(jnp.bfloat16)
    scaled = (anomalies / ((members - 1) * variance)).astype(jnp.bfloat16)
    return (scaled, obs_incr)


def adjust_kernel(prior_ref, values_ref, errors_ref, scaled_ref, incr_ref):
    scaled, obs_incr = adjust(prior_ref[...], values_ref[...][:, 0], errors_ref[...][:, 0])
    scaled_ref[...] = scaled
    incr_ref[...] = obs_incr


def adjust_rows(prior, values, errors, block=256):
    rows, members = prior.shape
    row_spec = pl.BlockSpec((block, members), lambda i: (i, 0))
    col_spec = pl.BlockSpec((block, 1), lambda i: (i, 0))
    out = jax.ShapeDtypeStruct((rows, members), jnp.bfloat16)
    return pl.pallas_call(
        adjust_kernel,
        grid=(rows // block,),
        in_specs=[row_spec, col_spec, col_spec],
        out_specs=[row_spec, row_spec],
        out_shape=[out, out],
    )(prior, values[:, None], errors[:, None])


def update_block(block_x, scaled, obs_incr, weights):
    centre = jnp.mean(block_x, axis=1, keepdims=True)
    state_anom = (block_x - centre).astype(jnp.bfloat16)
    linked = lax.dot_general(
        state_anom, scaled, (((1,), (1,)), ((), ())), preferred_element_type=jnp.float32
    )
    coupling = (linked * weights[None, :]).astype(jnp.bfloat16)
    return block_x + jnp.dot(coupling, obs_incr, preferred_element_type=jnp.float32)


def pick_owner(pieces, owners, axis):
    size = lax.axis_size(axis)
    me = lax.axis_index(axis)
    held = pieces
    step = 1
    while step < size:
        partner = lax.ppermute(held, axis, [(i, i ^ step) for i in range(size)])
        keep = ((me // step) % 2) == ((owners // step) % 2)
        held = jnp.where(keep[:, None, None], held, partner)
        step *= 2
    return held


def local(
    ensemble_state, obs_values, obs_error, batch_owner, readers, obs_order, obs_rows, loc_taper
):
    group_size = lax.axis_size("rows")
    region_count = lax.axis_size("region")
    region_idx = lax.axis_index("region")
    column_idx = lax.axis_index("rows")
    batches, obs_count = obs_order.shape
    slot_count = obs_count // group_size
    members = ensemble_state.shape[1]

    own_rows = lax.dynamic_slice_in_dim(obs_rows, column_idx * slot_count, slot_count, axis=1)
    pieces = ensemble_state[own_rows]
    pieces = pick_owner(pieces, batch_owner, "region")
    raw = lax.all_gather(pieces, "rows", axis=1, tiled=True)

    region_ids = jnp.arange(region_count, dtype=jnp.int32)
    reads = jnp.logical_or(
        region_ids[None, :] == batch_owner[:, None],
        jnp.any(readers[:, :, None] == region_ids[None, None, :], axis=1),
    )
    table = jnp.concatenate(
        [obs_values[:, :, None], obs_error[:, :, None], jnp.swapaxes(loc_taper, 1, 2)], axis=2
    )
    picks = (obs_order[:, :, None] == jnp.arange(obs_count, dtype=jnp.int32)).astype(jnp.float32)
    slot_table = jnp.einsum("bsj,bjc->bsc", picks, table, precision=lax.Precision.HIGHEST)
    slot_values = slot_table[:, :, 0]
    slot_errors = slot_table[:, :, 1]
    slot_taper = jnp.swapaxes(slot_table[:, :, 2 : 2 + region_count], 1, 2)

    pending = [raw[k] for k in range(batches)]
    scaled_list, incr_list = [], []
    for earlier in range(batches):
        scaled, obs_incr = adjust_rows(pending[earlier], slot_values[earlier], slot_errors[earlier])
        scaled_list.append(scaled)
        incr_list.append(obs_incr)
        later = list(range(earlier + 1, batches))
        if not later:
            break
        block_x = jnp.stack([pending[k] for k in later])
        weights = jnp.stack([slot_taper[earlier, batch_owner[k]] for k in later])
        applies = jnp.stack([reads[earlier, batch_owner[k]] for k in later])
        centre = jnp.mean(block_x, axis=2, keepdims=True)
        state_anom = (block_x - centre).astype(jnp.bfloat16)
        linked = jnp.einsum("kim,jm->kij", state_anom, scaled, preferred_element_type=jnp.float32)
        coupling = (linked * weights[:, None, :]).astype(jnp.bfloat16)
        moved = block_x + jnp.einsum("kij,jm->kim", coupling, obs_incr, preferred_element_type=jnp.float32)
        moved = jnp.where(applies[:, None, None], moved, block_x)
        for position, k in enumerate(later):
            pending[k] = moved[position]
    scaled_all = jnp.stack(scaled_list)
    incr_all = jnp.stack(incr_list)

    def main_step(batch_idx, current):
        weights = slot_taper[batch_idx, region_idx]
        return lax.cond(
            reads[batch_idx, region_idx],
            lambda rows_x: update_block(rows_x, scaled_all[batch_idx], incr_all[batch_idx], weights),
            lambda rows_x: rows_x,
            current,
        )

    current = lax.fori_loop(0, batches, main_step, ensemble_state)
    return current


def solution(mesh):
    placed = (P(("region", "rows"), None), P(), P(), P(), P(), P(), P(), P())
    return jax.shard_map(
        local, mesh=mesh, in_specs=placed, out_specs=P(("region", "rows"), None), check_vma=False
    )
```

profile of v0, /device:TPU:225, one launch (start us, length us, event | category | flops | bytes accessed | tf_op | source)
XLA Modules:
  0.0 167.2 jit_solution(13311528736953806743)
XLA Ops:
  6.5 3.1 %copy.55 = f32[2048,256]{1,0:T(8,128)} copy(f32[2048,256]{1,0:T(8,128)} %param.12) | data formatting | bytes 4194304
  9.6 0.8 compare_select_fusion
  10.5 2.3 %gather_fusion = f32[128,256]{1,0:T(8,128)S(1)} fusion(f32[2048,256]{1,0:T(8,128)} %copy.55, s32[1024]{0:T(1024)S(1)} %pad_clamp_fusion), kind=kCustom, calls=%fused_computation | custom fusion | bytes 262656 | tf_op jit(solution)/shard_map/gather | solution.py:78
  12.9 0.8 collective-permute-start
  13.7 3.6 %collective-permute-done = f32[4,32,256]{2,1,0:T(8,128)S(1)} collective-permute-done((f32[4,32,256]{2,1,0:T(8,128)S(1)}, f32[4,32,256]{2,1,0:T(8,128)S(1)}, u32[]{:S(2)}, u32[]{:S(2)}) %collective-permute-start) | collective-permute-done | bytes 131104 | tf_op jit(solution)/shard_map/ppermute | solution.py:59
  17.4 1.3 collective-permute-start.1
  18.7 7.5 %collective-permute-done.1 = f32[4,32,256]{2,1,0:T(8,128)S(1)} collective-permute-done((f32[4,32,256]{2,1,0:T(8,128)S(1)}, f32[4,32,256]{2,1,0:T(8,128)S(1)}, u32[]{:S(2)}, u32[]{:S(2)}) %collective-permute-start.1) | collective-permute-done | bytes 131104 | tf_op jit(solution)/shard_map/ppermute | solution.py:59
  26.3 1.3 collective-permute-start.2
  27.6 8.6 %collective-permute-done.2 = f32[4,32,256]{2,1,0:T(8,128)S(1)} collective-permute-done((f32[4,32,256]{2,1,0:T(8,128)S(1)}, f32[4,32,256]{2,1,0:T(8,128)S(1)}, u32[]{:S(2)}, u32[]{:S(2)}) %collective-permute-start.2) | collective-permute-done | bytes 131104 | tf_op jit(solution)/shard_map/ppermute | solution.py:59
  36.2 0.7 broadcast_select_fusion.2
  36.9 0.7 fusion.51
  41.7 8.3 %fusion.10 = f32[4,1024,10]{1,2,0:T(8,128)S(1)} fusion(s32[4,1024]{1,0:T(4,128)S(1)} %copy-done.12, f32[4,1024,8]{1,2,0:T(8,128)S(1)} %bitcast.105, f32[4,1024,1]{1,2,0:T(1,128)S(1)} %broadcast_in_dim.75, f32[4,1024,1]{1,2,0:T(1,128)S(1)} %broadcast_in_dim.74), kind=kOutput, calls=%fused_computation.13 | convolution fusion | flops 507592704 | bytes 344064 | tf_op jit(solution)/shard_map/bsj,bjc->bsc/dot_general | solution.py:91
  50.0 1.0 copy.26.values_ref
  51.1 1.0 copy.27.errors_ref
  52.1 1.0 copy.30.values_ref
  53.1 1.1 copy.31.errors_ref
  54.2 1.0 copy.34.values_ref
  55.2 1.0 copy.35.errors_ref
  56.3 1.1 copy.36.values_ref
  57.3 1.0 copy.37.errors_ref
  60.5 0.7 constant_dynamic-slice_fusion.8
  61.1 1.3 pad_add_fusion.1
  62.5 1.9 %pad_add_fusion = pred[3]{0:T(512)(128)(4,1)S(1)} fusion(pred[1]{0:T(512)(128)(4,1)} %bitcast.15, pred[1]{0:T(512)(128)(4,1)} %bitcast.13, pred[1]{0:T(512)(128)(4,1)} %bitcast.11), kind=kLoop, calls=%fused_computation.90 | loop fusion | flops 6 | bytes 6 | tf_op jit(solution)/shard_map/stack | solution.py:107
  64.4 24.1 %all-gather.2.cloned.1.call-done = f32[4,1024,256]{2,1,0:T(8,128)} async-done(((f32[4,32,256]{2,1,0:T(8,128)}), f32[4,1024,256]{2,1,0:T(8,128)}) %all-gather.2.cloned.1.call-update) | async-done | bytes 4194320 | tf_op jit(solution)/shard_map/all_gather | solution.py:80
  88.6 2.4 %slice_reduce_fusion = f32[3,1024]{1,0:T(4,128)S(1)} fusion(f32[4,1024,256]{2,1,0:T(8,128)} %all-gather.2.cloned.1.call-done), kind=kLoop, calls=%fused_computation.27 | loop fusion | flops 783360 | bytes 3158016 | tf_op jit(solution)/shard_map/reduce_sum | solution.py:108
  91.0 2.3 %slice_bitcast_fusion.2.prior_ref = f32[1024,256]{1,0:T(8,128)} fusion(f32[4,1024,256]{2,1,0:T(8,128)} %all-gather.2.cloned.1.call-done), kind=kLoop, calls=%fused_computation.39 | loop fusion | bytes 2097152 | tf_op jit(solution)/shard_map/squeeze | solution.py:96
  93.2 4.1 %shard_map.82 = (bf16[1024,256]{1,0:T(8,128)(2,1)}, bf16[1024,256]{1,0:T(8,128)(2,1)}) custom-call(f32[1024,256]{1,0:T(8,128)} %slice_bitcast_fusion.2.prior_ref, f32[1024,1]{1,0:T(8,128)} %copy.26.values_ref, f32[1024,1]{1,0:T(8,128)} %copy.27.errors_ref), custom_call_target="tpu_custom_call" | custom-call | tf_op jit(solution)/shard_map/pallas_call | solution.py:34
  97.4 6.8 %add_select_fusion = f32[3,1024,256]{2,1,0:T(8,128)S(1)} fusion(f32[4,1024,256]{2,1,0:T(8,128)} %all-gather.2.cloned.1.call-done, f32[3,1024]{1,0:T(4,128)S(1)} %pad_maximum_fusion.2, f32[3,1024]{1,0:T(4,128)S(1)} %broadcast_multiply_fusion.1, pred[3]{0:T(512)(128)(4,1)S(1)} %pad_add_fusion, bf16[1024,256]{1,0:T(8,128)(2,1)} %get-tuple-element.231, ...), kind=kOutput, calls=%fused_computation.19 | convolution fusion | flops 3230662656 | bytes 10510339 | tf_op jit(solution)/shard_map/kij,jm->kim/dot_general | solution.py:112
  104.5 1.0 slice_bitcast_fusion.1.prior_ref
  105.6 4.2 %shard_map.83 = (bf16[1024,256]{1,0:T(8,128)(2,1)}, bf16[1024,256]{1,0:T(8,128)(2,1)}) custom-call(f32[1024,256]{1,0:T(8,128)} %slice_bitcast_fusion.1.prior_ref, f32[1024,1]{1,0:T(8,128)} %copy.30.values_ref, f32[1024,1]{1,0:T(8,128)} %copy.31.errors_ref), custom_call_target="tpu_custom_call" | custom-call | tf_op jit(solution)/shard_map/pallas_call | solution.py:34
  109.7 5.0 %add_select_fusion.1 = f32[2,1024,256]{2,1,0:T(8,128)} fusion(f32[3,1024,256]{2,1,0:T(8,128)S(1)} %add_select_fusion, f32[2,1024]{1,0:T(2,128)S(1)} %pad_maximum_fusion.3, f32[2,1024]{1,0:T(2,128)S(1)} %broadcast_multiply_fusion.2, pred[2]{0:T(512)(128)(4,1)S(1)} %pad_add_fusion.1, bf16[1024,256]{1,0:T(8,128)(2,1)} %get-tuple-element.233, ...), kind=kOutput, calls=%fused_computation.24 | convolution fusion | flops 2153775104 | bytes 7356928 | tf_op jit(solution)/shard_map/kij,jm->kim/dot_general | solution.py:112
  114.8 2.9 %slice_reduce_fusion.2 = (f32[1024]{0:T(1024)S(1)}, f32[1024,256]{1,0:T(8,128)}) fusion(f32[2,1024,256]{2,1,0:T(8,128)} %add_select_fusion.1), kind=kLoop, calls=%fused_computation.42 | loop fusion | flops 261120 | bytes 3149824 | tf_op jit(solution)/shard_map/reduce_sum | solution.py:108
  117.6 4.1 %shard_map.84 = (bf16[1024,256]{1,0:T(8,128)(2,1)}, bf16[1024,256]{1,0:T(8,128)(2,1)}) custom-call(f32[1024,256]{1,0:T(8,128)} %get-tuple-element.254.prior_ref, f32[1024,1]{1,0:T(8,128)} %copy.34.values_ref, f32[1024,1]{1,0:T(8,128)} %copy.35.errors_ref), custom_call_target="tpu_custom_call" | custom-call | tf_op jit(solution)/shard_map/pallas_call | solution.py:34
  121.8 4.4 %fusion.24.prior_ref = f32[1024,256]{1,0:T(8,128)} fusion(bf16[1024,256]{1,0:T(8,128)(2,1)} %get-tuple-element.235, bf16[1024,256]{1,0:T(8,128)(2,1)} %get-tuple-element.234, f32[1024]{0:T(1024)S(1)} %bitcast.104, f32[2,1024,256]{2,1,0:T(8,128)S(1)} %copy-done, f32[1024]{0:T(1024)S(1)} %broadcast_multiply_fusion.3, pred[]{:T(512)} %bitcast.35), kind=kOutput, calls=%fused_computation.36 | convolution fusion | flops 1076887552 | bytes 4202497 | tf_op jit(solution)/shard_map/kij,jm->kim/dot_general | solution.py:112
  126.2 4.5 %shard_map.85 = (bf16[1024,256]{1,0:T(8,128)(2,1)}, bf16[1024,256]{1,0:T(8,128)(2,1)}) custom-call(f32[1024,256]{1,0:T(8,128)} %fusion.24.prior_ref, f32[1024,1]{1,0:T(8,128)} %copy.36.values_ref, f32[1024,1]{1,0:T(8,128)} %copy.37.errors_ref), custom_call_target="tpu_custom_call" | custom-call | tf_op jit(solution)/shard_map/pallas_call | solution.py:34
  130.7 3.3 %pad_maximum_fusion = (bf16[4,1024,256]{2,1,0:T(8,128)(2,1)}, bf16[4,1024,256]{2,1,0:T(8,128)(2,1)}) fusion(bf16[1,1024,256]{2,1,0:T(8,128)(2,1)} %bitcast.99, bf16[1,1024,256]{2,1,0:T(8,128)(2,1)S(1)} %bitcast.97, bf16[1,1024,256]{2,1,0:T(8,128)(2,1)S(1)} %bitcast.95, bf16[1,1024,256]{2,1,0:T(8,128)(2,1)S(1)} %bitcast.93, ...), kind=kLoop, calls=%fused_computation.28 | loop fusion | flops 6291456 | bytes 8388608 | tf_op jit(solution)/shard_map/stack | solution.py:116
  134.0 26.4 %while.18 = (s32[]{:T(128)}, f32[2048,256]{1,0:T(8,128)}, pred[4,8]{1,0:T(4,128)(4,1)S(1)}, s32[]{:T(128)}, bf16[4,1024,256]{2,1,0:T(8,128)(2,1)}, /*index=5*/f3...) while((s32[]{:T(128)}, f32[2048,256]{1,0:T(8,128)}, pred[4,8]{1,0:T(4,128)(4,1)S(1)}, ...), condition=%wide.region_8.9_spmd, body=%wide.region_4.8_spmd.sunk | while | flops 2153775104 | bytes 13677774 | solution.py:128
  134.0 0.6 dynamic_slice.82
  135.3 7.0 %conditional.2 = (f32[2048,256]{1,0:T(8,128)}) conditional(s32[]{:T(128)} %bitcast.92, f32[2048,256]{1,0:T(8,128)} %get-tuple-element.337, (f32[2048,256]{1,0:T(8,128)}, s32[]{:T(128)}, bf16[4,1024,256]{2,1,0:T(8,128)(2,1)}, f32[4,8,1024]{2,1,0:T(8,128)S(1)}, s32[]{:T(128)}, /*index=5*/bf16[4,1024,256]{2,1,0:T(8,128)(2,1)}) %tuple.74), branch_computations={%region_5.5_spmd, %region_6.7_spmd} | conditional | flops 2153775104 | bytes 13677622 | solution.py:121
  135.3 1.6 copy.52
  137.3 5.0 %convolution_add_fusion = f32[2048,256]{1,0:T(8,128)} fusion(f32[2048,256]{1,0:T(8,128)S(1)} %copy.52, f32[1024]{0:T(1024)S(1)} %bitcast.103, f32[2048]{0:T(1024)S(1)} %broadcast_multiply_fusion, bf16[4,1024,256]{2,1,0:T(8,128)(2,1)} %get-tuple-element.212, s32[]{:T(128)S(6)} %select_n.92, bf16[4,1024,256]{2,1,0:T(8,128)(2,1)} %get-tuple-element.208), kind=kOutput, calls=%fused_computation.2 | convolution fusion | flops 2153250816 | bytes 7353344 | tf_op jit(solution)/shard_map/while/body/eval_jaxpr/cond/branch_1_fun/dot_general | solution.py:50
  143.7 0.7 dynamic_slice.82
  145.0 7.0 %conditional.2 = (f32[2048,256]{1,0:T(8,128)}) conditional(s32[]{:T(128)} %bitcast.92, f32[2048,256]{1,0:T(8,128)} %get-tuple-element.337, (f32[2048,256]{1,0:T(8,128)}, s32[]{:T(128)}, bf16[4,1024,256]{2,1,0:T(8,128)(2,1)}, f32[4,8,1024]{2,1,0:T(8,128)S(1)}, s32[]{:T(128)}, /*index=5*/bf16[4,1024,256]{2,1,0:T(8,128)(2,1)}) %tuple.74), branch_computations={%region_5.5_spmd, %region_6.7_spmd} | conditional | flops 2153775104 | bytes 13677622 | solution.py:121
  145.0 1.6 copy.52
  147.0 5.0 %convolution_add_fusion = f32[2048,256]{1,0:T(8,128)} fusion(f32[2048,256]{1,0:T(8,128)S(1)} %copy.52, f32[1024]{0:T(1024)S(1)} %bitcast.103, f32[2048]{0:T(1024)S(1)} %broadcast_multiply_fusion, bf16[4,1024,256]{2,1,0:T(8,128)(2,1)} %get-tuple-element.212, s32[]{:T(128)S(6)} %select_n.92, bf16[4,1024,256]{2,1,0:T(8,128)(2,1)} %get-tuple-element.208), kind=kOutput, calls=%fused_computation.2 | convolution fusion | flops 2153250816 | bytes 7353344 | tf_op jit(solution)/shard_map/while/body/eval_jaxpr/cond/branch_1_fun/dot_general | solution.py:50
  153.3 7.0 %conditional.2 = (f32[2048,256]{1,0:T(8,128)}) conditional(s32[]{:T(128)} %bitcast.92, f32[2048,256]{1,0:T(8,128)} %get-tuple-element.337, (f32[2048,256]{1,0:T(8,128)}, s32[]{:T(128)}, bf16[4,1024,256]{2,1,0:T(8,128)(2,1)}, f32[4,8,1024]{2,1,0:T(8,128)S(1)}, s32[]{:T(128)}, /*index=5*/bf16[4,1024,256]{2,1,0:T(8,128)(2,1)}) %tuple.74), branch_computations={%region_5.5_spmd, %region_6.7_spmd} | conditional | flops 2153775104 | bytes 13677622 | solution.py:121
  153.3 1.6 copy.52
  155.3 5.0 %convolution_add_fusion = f32[2048,256]{1,0:T(8,128)} fusion(f32[2048,256]{1,0:T(8,128)S(1)} %copy.52, f32[1024]{0:T(1024)S(1)} %bitcast.103, f32[2048]{0:T(1024)S(1)} %broadcast_multiply_fusion, bf16[4,1024,256]{2,1,0:T(8,128)(2,1)} %get-tuple-element.212, s32[]{:T(128)S(6)} %select_n.92, bf16[4,1024,256]{2,1,0:T(8,128)(2,1)} %get-tuple-element.208), kind=kOutput, calls=%fused_computation.2 | convolution fusion | flops 2153250816 | bytes 7353344 | tf_op jit(solution)/shard_map/while/body/eval_jaxpr/cond/branch_1_fun/dot_general | solution.py:50
  (59 shorter events, 3.5 us)
Async XLA Ops:
  6.5 7.2 %copy-start.9 = (s32[4]{0:T(128)S(1)}, s32[4]{0:T(128)}, u32[]{:S(2)}) copy-start(s32[4]{0:T(128)} %param.15) | copy-start | bytes 52
  6.5 82.1 %all-gather.2.cloned.1.call-start = ((), (), s32[]{:S(2)}) async-start(), calls=%async_computation | async-start | bytes 4325376 | tf_op jit(solution)/shard_map/all_gather | solution.py:80
  9.6 31.9 %copy-start.10 = (s32[4,3]{1,0:T(4,128)S(1)}, s32[4,3]{1,0:T(4,128)}, u32[]{:S(2)}) copy-start(s32[4,3]{1,0:T(4,128)} %param.16) | copy-start | bytes 148
  9.6 32.0 %copy-start.7 = (f32[4,1024]{1,0:T(4,128)S(1)}, f32[4,1024]{1,0:T(4,128)}, u32[]{:S(2)}) copy-start(f32[4,1024]{1,0:T(4,128)} %param.14) | copy-start | bytes 49156
  9.6 32.0 %copy-start.8 = (f32[4,1024]{1,0:T(4,128)S(1)}, f32[4,1024]{1,0:T(4,128)}, u32[]{:S(2)}) copy-start(f32[4,1024]{1,0:T(4,128)} %param.13) | copy-start | bytes 49156
  9.6 32.0 %copy-start.11 = (f32[4,8,1024]{2,1,0:T(8,128)S(1)}, f32[4,8,1024]{2,1,0:T(8,128)}, u32[]{:S(2)}) copy-start(f32[4,8,1024]{2,1,0:T(8,128)} %param.19) | copy-start | bytes 393220
  9.6 32.0 %copy-start.12 = (s32[4,1024]{1,0:T(4,128)S(1)}, s32[4,1024]{1,0:T(4,128)}, u32[]{:S(2)}) copy-start(s32[4,1024]{1,0:T(4,128)} %param.17) | copy-start | bytes 49156
  12.9 4.5 %collective-permute-start = (f32[4,32,256]{2,1,0:T(8,128)S(1)}, f32[4,32,256]{2,1,0:T(8,128)S(1)}, u32[]{:S(2)}, u32[]{:S(2)}) collective-permute-start(f32[4,32,256]{2,1,0:T(8,128)S(1)} %bitcast.101), channel_id=1, source_target_pairs={{0,32},{32,0},{64,96},{96,64},{128,160},{160,128},{192,224},{224,1... | collective-permute-start | bytes 393224 | tf_op jit(solution)/shard_map/ppermute | solution.py:59
  17.4 8.7 %collective-permute-start.1 = (f32[4,32,256]{2,1,0:T(8,128)S(1)}, f32[4,32,256]{2,1,0:T(8,128)S(1)}, u32[]{:S(2)}, u32[]{:S(2)}) collective-permute-start(f32[4,32,256]{2,1,0:T(8,128)S(1)} %broadcast_select_fusion), channel_id=1, source_target_pairs={{0,64},{32,96},{64,0},{96,32},{128,192},{160,224},{192,128},{224,1... | collective-permute-start | bytes 393224 | tf_op jit(solution)/shard_map/ppermute | solution.py:59
  26.3 9.9 %collective-permute-start.2 = (f32[4,32,256]{2,1,0:T(8,128)S(1)}, f32[4,32,256]{2,1,0:T(8,128)S(1)}, u32[]{:S(2)}, u32[]{:S(2)}) collective-permute-start(f32[4,32,256]{2,1,0:T(8,128)S(1)} %broadcast_select_fusion.1), channel_id=1, source_target_pairs={{0,128},{32,160},{64,192},{96,224},{128,0},{160,32},{192,64},{224,... | collective-permute-start | bytes 393224 | tf_op jit(solution)/shard_map/ppermute | solution.py:59
  114.8 7.0 %copy-start = (f32[2,1024,256]{2,1,0:T(8,128)S(1)}, f32[2,1024,256]{2,1,0:T(8,128)}, u32[]{:S(2)}) copy-start(f32[2,1024,256]{2,1,0:T(8,128)} %add_select_fusion.1) | copy-start | bytes 6291460
  121.8 8.9 %copy-start.5 = (bf16[1024,256]{1,0:T(8,128)(2,1)S(1)}, bf16[1024,256]{1,0:T(8,128)(2,1)}, u32[]{:S(2)}) copy-start(bf16[1024,256]{1,0:T(8,128)(2,1)} %get-tuple-element.234) | copy-start | bytes 1572868
  121.8 8.9 %copy-start.6 = (bf16[1024,256]{1,0:T(8,128)(2,1)S(1)}, bf16[1024,256]{1,0:T(8,128)(2,1)}, u32[]{:S(2)}) copy-start(bf16[1024,256]{1,0:T(8,128)(2,1)} %get-tuple-element.235) | copy-start | bytes 1572868
  126.1 4.5 %copy-start.1 = (bf16[1024,256]{1,0:T(8,128)(2,1)S(1)}, bf16[1024,256]{1,0:T(8,128)(2,1)}, u32[]{:S(2)}) copy-start(bf16[1024,256]{1,0:T(8,128)(2,1)} %get-tuple-element.230) | copy-start | bytes 1572868
  126.2 4.5 %copy-start.2 = (bf16[1024,256]{1,0:T(8,128)(2,1)S(1)}, bf16[1024,256]{1,0:T(8,128)(2,1)}, u32[]{:S(2)}) copy-start(bf16[1024,256]{1,0:T(8,128)(2,1)} %get-tuple-element.231) | copy-start | bytes 1572868
  126.2 4.5 %copy-start.3 = (bf16[1024,256]{1,0:T(8,128)(2,1)S(1)}, bf16[1024,256]{1,0:T(8,128)(2,1)}, u32[]{:S(2)}) copy-start(bf16[1024,256]{1,0:T(8,128)(2,1)} %get-tuple-element.232) | copy-start | bytes 1572868
  126.2 4.5 %copy-start.4 = (bf16[1024,256]{1,0:T(8,128)(2,1)S(1)}, bf16[1024,256]{1,0:T(8,128)(2,1)}, u32[]{:S(2)}) copy-start(bf16[1024,256]{1,0:T(8,128)(2,1)} %get-tuple-element.233) | copy-start | bytes 1572868
Sparse Core Ops, SparseCore 0:
  37.1 51.4 all-gather.1
where the time goes:
time: 169 us; the launch traced here: 167 us
  waiting for transfers between devices  43.8 us (26%)
  matrix products  39.5 us (23%)
  local copies, waits for them, and re-layouts  26.1 us (15%)
  between operations  19.5 us (12%)
  Pallas kernels  16.9 us (10%)
  other arithmetic  15 us (9%)
  starting transfers between devices  3.4 us (2%)
  loops' own time  2.87 us (2%)
    all_gather x1, waiting for transfers between devices, local(): raw = lax.all_gather(pieces, 'rows', axis=1, tiled=True)  24.1 us
    ppermute x3, waiting for transfers between devices, pick_owner(): partner = lax.ppermute(held, axis, [(i, i ^ step) for i in range(size)])  19.7 us
    pallas_call x4, Pallas kernels, adjust_rows(): pl.pallas_call(adjust_kernel, grid=(rows // block,), in_specs=[row_spec,...  16.9 us
    dot_general x3, matrix products, local(): jnp.einsum('kij,jm->kim', coupling, obs_incr, preferred_element_type=jnp....  16.2 us
    dot_general x3, matrix products, update_block(): jnp.dot(coupling, obs_incr, preferred_element_type=jnp.float32)  15.1 us
    dot_general x1, matrix products, local(): jnp.einsum('bsj,bjc->bsc', picks, table, precision=lax.Precision.HIGHEST)  8.32 us
    reduce_sum x3, other arithmetic, local(): centre = jnp.mean(block_x, axis=2, keepdims=True)  5.58 us
    cond x3, local copies, waits for them, and re-layouts  4.78 us
  transfers between devices with their start and end apart: 4, of which 4 were waited for; matrix products, arithmetic and copies ran while one was open for 13% of the time, Pallas kernels for 0%

commit v1 on v0

--- a/solution.py
+++ b/solution.py
@@ -48,6 +48,35 @@
     )
     coupling = (linked * weights[None, :]).astype(jnp.bfloat16)
     return block_x + jnp.dot(coupling, obs_incr, preferred_element_type=jnp.float32)
+
+
+def update_kernel(x_ref, scaled_ref, incr_ref, weights_ref, out_ref):
+    current = x_ref[...]
+    for batch_idx in range(scaled_ref.shape[0]):
+        centre = jnp.mean(current, axis=1, keepdims=True)
+        state_anom = (current - centre).astype(jnp.bfloat16)
+        linked = lax.dot_general(
+            state_anom, scaled_ref[batch_idx], (((1,), (1,)), ((), ())),
+            preferred_element_type=jnp.float32,
+        )
+        coupling = (linked * weights_ref[0, batch_idx]).astype(jnp.bfloat16)
+        current = current + jnp.dot(coupling, incr_ref[batch_idx], preferred_element_type=jnp.float32)
+    out_ref[...] = current
+
+
+def update_rows(block_x, scaled, obs_incr, weights, group_rows, block=256):
+    rows, members = block_x.shape
+    row_spec = pl.BlockSpec((block, members), lambda i: (i, 0))
+    full_spec = pl.BlockSpec(scaled.shape, lambda i: (0, 0, 0))
+    per_group = group_rows // block
+    weight_spec = pl.BlockSpec((1,) + weights.shape[1:], lambda i: (i // per_group, 0, 0, 0))
+    return pl.pallas_call(
+        update_kernel,
+        grid=(rows // block,),
+        in_specs=[row_spec, full_spec, full_spec, weight_spec],
+        out_specs=row_spec,
+        out_shape=jax.ShapeDtypeStruct(block_x.shape, block_x.dtype),
+    )(block_x, scaled, obs_incr, weights)
 
 
 def pick_owner(pieces, owners, axis):
@@ -102,30 +131,25 @@
         later = list(range(earlier + 1, batches))
         if not later:
             break
-        block_x = jnp.stack([pending[k] for k in later])
-        weights = jnp.stack([slot_taper[earlier, batch_owner[k]] for k in later])
-        applies = jnp.stack([reads[earlier, batch_owner[k]] for k in later])
-        centre = jnp.mean(block_x, axis=2, keepdims=True)
-        state_anom = (block_x - centre).astype(jnp.bfloat16)
-        linked = jnp.einsum("kim,jm->kij", state_anom, scaled, preferred_element_type=jnp.float32)
-        coupling = (linked * weights[:, None, :]).astype(jnp.bfloat16)
-        moved = block_x + jnp.einsum("kij,jm->kim", coupling, obs_incr, preferred_element_type=jnp.float32)
-        moved = jnp.where(applies[:, None, None], moved, block_x)
+        block_x = jnp.concatenate([pending[k] for k in later])
+        weights = jnp.stack(
+            [
+                jnp.where(reads[earlier, batch_owner[k]], slot_taper[earlier, batch_owner[k]], 0.0)
+                for k in later
+            ]
+        )
+        moved = update_rows(
+            block_x, scaled[None], obs_incr[None], weights[:, None, None, :], obs_count
+        ).reshape(len(later), obs_count, members)
         for position, k in enumerate(later):
             pending[k] = moved[position]
     scaled_all = jnp.stack(scaled_list)
     incr_all = jnp.stack(incr_list)
 
-    def main_step(batch_idx, current):
-        weights = slot_taper[batch_idx, region_idx]
-        return lax.cond(
-            reads[batch_idx, region_idx],
-            lambda rows_x: update_block(rows_x, scaled_all[batch_idx], incr_all[batch_idx], weights),
-            lambda rows_x: rows_x,
-            current,
-        )
-
-    current = lax.fori_loop(0, batches, main_step, ensemble_state)
+    main_weights = jnp.where(reads[:, region_idx, None], slot_taper[:, region_idx], 0.0)
+    current = update_rows(
+        ensemble_state, scaled_all, incr_all, main_weights[None, :, None, :], ensemble_state.shape[0]
+    )
     return current
 
 

time: 169 us -> 176 us (1.041)
  the two profiles are of different devices: /device:TPU:225 before, /device:TPU:1 now
where the time goes in v1:
time: 176 us; the launch traced here: 175 us
  Pallas kernels  62.2 us (35%)
  waiting for transfers between devices  34.3 us (19%)
  local copies, waits for them, and re-layouts  25.6 us (15%)
  between operations  19.1 us (11%)
  starting transfers between devices  12.9 us (7%)
  other arithmetic  12.7 us (7%)
  matrix products  8.14 us (5%)
    pallas_call x4, Pallas kernels, update_rows(): pl.pallas_call(update_kernel, grid=(rows // block,), in_specs=[row_spec,...  45.6 us
    all_gather x1, waiting for transfers between devices, local(): raw = lax.all_gather(pieces, 'rows', axis=1, tiled=True)  24 us
    pallas_call x4, Pallas kernels, adjust_rows(): pl.pallas_call(adjust_kernel, grid=(rows // block,), in_specs=[row_spec,...  16.7 us
    ppermute x3, starting transfers between devices, pick_owner(): partner = lax.ppermute(held, axis, [(i, i ^ step) for i in range(size)])  12.9 us
    ppermute x3, waiting for transfers between devices, pick_owner(): partner = lax.ppermute(held, axis, [(i, i ^ step) for i in range(size)])  10.3 us
    dot_general x1, matrix products, local(): jnp.einsum('bsj,bjc->bsc', picks, table, precision=lax.Precision.HIGHEST)  8.14 us
    slice x2, local copies, waits for them, and re-layouts, local(): pending[k] = moved[position]  5.29 us
    select_n x1, other arithmetic, local(): jnp.where(reads[earlier, batch_owner[k]], slot_taper[earlier, batch_owner...  4.36 us
  transfers between devices with their start and end apart: 4, of which 4 were waited for; matrix products, arithmetic and copies ran while one was open for 14% of the time, Pallas kernels for 0%

profile of v1, /device:TPU:1, one launch (start us, length us, event | category | flops | bytes accessed | tf_op | source)
XLA Modules:
  0.0 175.1 jit_solution(2559349683162736642)
XLA Ops:
  6.5 0.0 all-gather.2.cloned.1.call-start
  6.6 0.8 compare_select_fusion
  7.4 0.1 reshape.162
  7.5 2.3 %gather_fusion = f32[128,256]{1,0:T(8,128)S(1)} fusion(f32[2048,256]{1,0:T(8,128)} %x_ref.1, s32[1024]{0:T(1024)S(1)} %pad_clamp_fusion), kind=kCustom, calls=%fused_computation | custom fusion | bytes 262656 | tf_op jit(solution)/shard_map/gather | solution.py:107
  9.9 2.5 %collective-permute-start = (f32[4,32,256]{2,1,0:T(8,128)S(1)}, f32[4,32,256]{2,1,0:T(8,128)S(1)}, u32[]{:S(2)}, u32[]{:S(2)}) collective-permute-start(f32[4,32,256]{2,1,0:T(8,128)S(1)} %bitcast.71), channel_id=1, source_target_pairs={{0,32},{32,0},{64,96},{96,64},{128,160},{160,128},{192,224},{224,1... | collective-permute-start | bytes 393224 | tf_op jit(solution)/shard_map/ppermute | solution.py:88
  12.4 0.7 fusion.16
  13.1 1.7 collective-permute-done
  14.8 0.1 broadcast_select_fusion
  14.8 3.8 %collective-permute-start.1 = (f32[4,32,256]{2,1,0:T(8,128)S(1)}, f32[4,32,256]{2,1,0:T(8,128)S(1)}, u32[]{:S(2)}, u32[]{:S(2)}) collective-permute-start(f32[4,32,256]{2,1,0:T(8,128)S(1)} %broadcast_select_fusion), channel_id=1, source_target_pairs={{0,64},{32,96},{64,0},{96,32},{128,192},{160,224},{192,128},{224,1... | collective-permute-start | bytes 393224 | tf_op jit(solution)/shard_map/ppermute | solution.py:88
  18.7 5.8 %collective-permute-done.1 = f32[4,32,256]{2,1,0:T(8,128)S(1)} collective-permute-done((f32[4,32,256]{2,1,0:T(8,128)S(1)}, f32[4,32,256]{2,1,0:T(8,128)S(1)}, u32[]{:S(2)}, u32[]{:S(2)}) %collective-permute-start.1) | collective-permute-done | bytes 131104 | tf_op jit(solution)/shard_map/ppermute | solution.py:88
  24.4 0.1 broadcast_select_fusion.1
  24.5 6.5 %collective-permute-start.2 = (f32[4,32,256]{2,1,0:T(8,128)S(1)}, f32[4,32,256]{2,1,0:T(8,128)S(1)}, u32[]{:S(2)}, u32[]{:S(2)}) collective-permute-start(f32[4,32,256]{2,1,0:T(8,128)S(1)} %broadcast_select_fusion.1), channel_id=1, source_target_pairs={{0,128},{32,160},{64,192},{96,224},{128,0},{160,32},{192,64},{224,... | collective-permute-start | bytes 393224 | tf_op jit(solution)/shard_map/ppermute | solution.py:88
  31.0 2.9 %collective-permute-done.2 = f32[4,32,256]{2,1,0:T(8,128)S(1)} collective-permute-done((f32[4,32,256]{2,1,0:T(8,128)S(1)}, f32[4,32,256]{2,1,0:T(8,128)S(1)}, u32[]{:S(2)}, u32[]{:S(2)}) %collective-permute-start.2) | collective-permute-done | bytes 131104 | tf_op jit(solution)/shard_map/ppermute | solution.py:88
  33.9 0.7 broadcast_select_fusion.2
  34.7 0.7 fusion.23
  39.1 8.1 %fusion = f32[4,1024,10]{1,2,0:T(8,128)S(1)} fusion(s32[4,1024]{1,0:T(4,128)S(1)} %copy-done.11, f32[4,1024,8]{1,2,0:T(8,128)S(1)} %bitcast.73, f32[4,1024,1]{1,2,0:T(1,128)S(1)} %broadcast_in_dim.81, f32[4,1024,1]{1,2,0:T(1,128)S(1)} %broadcast_in_dim.80), kind=kOutput, calls=%fused_computation.2 | convolution fusion | flops 507592704 | bytes 344064 | tf_op jit(solution)/shard_map/bsj,bjc->bsc/dot_general | solution.py:120
  47.3 1.0 copy.17.values_ref
  48.4 1.0 copy.18.errors_ref
  49.4 0.1 copy.19
  51.3 0.1 fusion.7
  51.4 0.1 fusion.14
  51.5 0.7 constant_dynamic-slice_fusion.7
  52.2 4.4 %fusion.13 = (f32[1,1,1,1024]{3,2,1,0:T(1,128)}, f32[1,1024]{1,0:T(1,128)S(1)}, f32[1,1024]{1,0:T(1,128)S(1)}, f32[1,1024]{1,0:T(1,128)S(1)}, f32[1,1024]{1,0:T(1,128)S(1)}, /*index=5*/f32[1,1024]{1,0:T(1,128)S(1)}) fusion(pred[]{:T(512)} %bitcast.31, f32[4,1024,8]{1,2,0:T(8,128)S(1)} %slice.119, s32[]{:T(128)S(6)} %select_n.216, pred[]{:T(512)} %bitcast.25, ...), kind=kLoop, calls=%fused_computation.36 | loop fusion | flops 6144 | bytes 49170 | tf_op jit(solution)/shard_map/jit(_where)/select_n | solution.py:137
  56.6 0.6 broadcast_in_dim.84.weights_ref
  57.2 1.0 copy.20.values_ref
  58.2 1.1 copy.21.errors_ref
  59.3 0.6 broadcast_in_dim.86.weights_ref
  59.9 1.1 copy.22.values_ref
  61.0 1.0 copy.23.errors_ref
  62.0 1.0 copy.24.values_ref
  63.0 1.1 copy.25.errors_ref
  64.1 0.2 fusion.15
  64.3 0.7 broadcast_select_fusion.3.weights_ref
  65.0 24.0 %all-gather.2.cloned.1.call-done = f32[4,1024,256]{2,1,0:T(8,128)} async-done(((f32[4,32,256]{2,1,0:T(8,128)}), f32[4,1024,256]{2,1,0:T(8,128)}) %all-gather.2.cloned.1.call-update) | async-done | bytes 4194320 | tf_op jit(solution)/shard_map/all_gather | solution.py:109
  88.9 3.5 %slice_bitcast_fusion.3 = (f32[1024,256]{1,0:T(8,128)}, f32[1024,256]{1,0:T(8,128)S(1)}, f32[1024,256]{1,0:T(8,128)S(1)}, f32[1024,256]{1,0:T(8,128)S(1)}) fusion(f32[4,1024,256]{2,1,0:T(8,128)} %all-gather.2.cloned.1.call-done), kind=kLoop, calls=%fused_computation.10 | loop fusion | bytes 8388608 | tf_op jit(solution)/shard_map/squeeze | solution.py:125
  92.5 1.8 %pad_maximum_fusion.x_ref = f32[3072,256]{1,0:T(8,128)} fusion(f32[1024,256]{1,0:T(8,128)S(1)} %get-tuple-element.22, f32[1024,256]{1,0:T(8,128)S(1)} %get-tuple-element.23, f32[1024,256]{1,0:T(8,128)S(1)} %get-tuple-element.24), kind=kLoop, calls=%fused_computation.4 | loop fusion | flops 1572864 | bytes 6291456 | tf_op jit(solution)/shard_map/concatenate | solution.py:134
  94.3 4.2 %shard_map.82 = (bf16[1024,256]{1,0:T(8,128)(2,1)}, bf16[1024,256]{1,0:T(8,128)(2,1)}) custom-call(f32[1024,256]{1,0:T(8,128)} %get-tuple-element.21.prior_ref, f32[1024,1]{1,0:T(8,128)} %copy.17.values_ref, f32[1024,1]{1,0:T(8,128)} %copy.18.errors_ref), custom_call_target="tpu_custom_call" | custom-call | tf_op jit(solution)/shard_map/pallas_call | solution.py:34
  98.4 11.6 %shard_map.83 = f32[3072,256]{1,0:T(8,128)} custom-call(f32[3072,256]{1,0:T(8,128)} %pad_maximum_fusion.x_ref, bf16[1,1024,256]{2,1,0:T(8,128)(2,1)} %bitcast.65, bf16[1,1024,256]{2,1,0:T(8,128)(2,1)} %bitcast.67, f32[3,1,1,1024]{3,2,1,0:T(1,128)} %broadcast_in_dim.84.weights_ref), custom_call_target="tpu_custom_call" | custom-call | tf_op jit(solution)/shard_map/pallas_call | solution.py:73
  110.0 2.3 %slice.120.prior_ref = f32[1024,256]{1,0:T(8,128)} slice(f32[3072,256]{1,0:T(8,128)} %shard_map.83), slice={[0:1024], [0:256]} | slice | bytes 2097152 | tf_op jit(solution)/shard_map/slice | solution.py:145
  112.3 3.0 %concatenate.12.x_ref = f32[2048,256]{1,0:T(8,128)} slice(f32[3072,256]{1,0:T(8,128)} %shard_map.83), slice={[1024:3072], [0:256]} | slice | bytes 4194304 | tf_op jit(solution)/shard_map/concatenate | solution.py:134
  115.4 4.2 %shard_map.84 = (bf16[1024,256]{1,0:T(8,128)(2,1)}, bf16[1024,256]{1,0:T(8,128)(2,1)}) custom-call(f32[1024,256]{1,0:T(8,128)} %slice.120.prior_ref, f32[1024,1]{1,0:T(8,128)} %copy.20.values_ref, f32[1024,1]{1,0:T(8,128)} %copy.21.errors_ref), custom_call_target="tpu_custom_call" | custom-call | tf_op jit(solution)/shard_map/pallas_call | solution.py:34
  119.5 8.3 %shard_map.85 = f32[2048,256]{1,0:T(8,128)} custom-call(f32[2048,256]{1,0:T(8,128)} %concatenate.12.x_ref, bf16[1,1024,256]{2,1,0:T(8,128)(2,1)} %bitcast.57, bf16[1,1024,256]{2,1,0:T(8,128)(2,1)} %bitcast.59, f32[2,1,1,1024]{3,2,1,0:T(1,128)} %broadcast_in_dim.86.weights_ref), custom_call_target="tpu_custom_call" | custom-call | tf_op jit(solution)/shard_map/pallas_call | solution.py:73
  127.8 3.0 %fusion.22 = (f32[1024,256]{1,0:T(8,128)}, f32[1024,256]{1,0:T(8,128)}) fusion(f32[2048,256]{1,0:T(8,128)} %shard_map.85), kind=kLoop, calls=%fused_computation.78 | loop fusion | bytes 4194304 | tf_op jit(solution)/shard_map/slice | solution.py:145
  130.8 4.2 %shard_map.86 = (bf16[1024,256]{1,0:T(8,128)(2,1)}, bf16[1024,256]{1,0:T(8,128)(2,1)}) custom-call(f32[1024,256]{1,0:T(8,128)} %get-tuple-element.25.prior_ref, f32[1024,1]{1,0:T(8,128)} %copy.22.values_ref, f32[1024,1]{1,0:T(8,128)} %copy.23.errors_ref), custom_call_target="tpu_custom_call" | custom-call | tf_op jit(solution)/shard_map/pallas_call | solution.py:34
  135.0 5.1 %shard_map.87.prior_ref = f32[1024,256]{1,0:T(8,128)} custom-call(f32[1024,256]{1,0:T(8,128)} %get-tuple-element.26.x_ref, bf16[1,1024,256]{2,1,0:T(8,128)(2,1)} %bitcast.61, bf16[1,1024,256]{2,1,0:T(8,128)(2,1)} %bitcast.63, f32[1,1,1,1024]{3,2,1,0:T(1,128)} %get-tuple-element.35.weights_ref), custom_call_target="tpu_custom_call" | custom-call | tf_op jit(solution)/shard_map/pallas_call | solution.py:73
  140.0 4.2 %shard_map.88 = (bf16[1024,256]{1,0:T(8,128)(2,1)}, bf16[1024,256]{1,0:T(8,128)(2,1)}) custom-call(f32[1024,256]{1,0:T(8,128)} %shard_map.87.prior_ref, f32[1024,1]{1,0:T(8,128)} %copy.24.values_ref, f32[1024,1]{1,0:T(8,128)} %copy.25.errors_ref), custom_call_target="tpu_custom_call" | custom-call | tf_op jit(solution)/shard_map/pallas_call | solution.py:34
  144.3 3.3 %pad_maximum_fusion.1 = (bf16[4,1024,256]{2,1,0:T(8,128)(2,1)}, bf16[4,1024,256]{2,1,0:T(8,128)(2,1)}) fusion(bf16[1,1024,256]{2,1,0:T(8,128)(2,1)} %bitcast.69, bf16[1,1024,256]{2,1,0:T(8,128)(2,1)S(1)} %bitcast.62, bf16[1,1024,256]{2,1,0:T(8,128)(2,1)S(1)} %bitcast.58, bf16[1,1024,256]{2,1,0:T(8,128)(2,1)S(1)} %bitcast.66, ...), kind=kLoop, calls=%fused_computation.5 | loop fusion | flops 6291456 | bytes 8388608 | tf_op jit(solution)/shard_map/stack | solution.py:146
  147.6 20.7 %shard_map.89 = f32[2048,256]{1,0:T(8,128)} custom-call(f32[2048,256]{1,0:T(8,128)} %x_ref.1, bf16[4,1024,256]{2,1,0:T(8,128)(2,1)} %get-tuple-element.53.scaled_ref, bf16[4,1024,256]{2,1,0:T(8,128)(2,1)} %get-tuple-element.54.incr_ref, f32[1,4,1,1024]{3,2,1,0:T(1,128)} %broadcast_select_fusion.3.weights_ref), custom_call_target="tpu_custom_call" | custom-call | tf_op jit(solution)/shard_map/pallas_call | solution.py:73
  (32 shorter events, 0.2 us)
Async XLA Ops:
  6.5 28.2 %copy-start.8 = (s32[4]{0:T(128)S(1)}, s32[4]{0:T(128)}, u32[]{:S(2)}) copy-start(s32[4]{0:T(128)} %param.11) | copy-start | bytes 52
  6.5 32.5 %copy-start.6 = (f32[4,1024]{1,0:T(4,128)S(1)}, f32[4,1024]{1,0:T(4,128)}, u32[]{:S(2)}) copy-start(f32[4,1024]{1,0:T(4,128)} %param.9) | copy-start | bytes 49156
  6.5 32.5 %copy-start.7 = (f32[4,1024]{1,0:T(4,128)S(1)}, f32[4,1024]{1,0:T(4,128)}, u32[]{:S(2)}) copy-start(f32[4,1024]{1,0:T(4,128)} %param.10) | copy-start | bytes 49156
  6.5 32.5 %copy-start.10 = (f32[4,8,1024]{2,1,0:T(8,128)S(1)}, f32[4,8,1024]{2,1,0:T(8,128)}, u32[]{:S(2)}) copy-start(f32[4,8,1024]{2,1,0:T(8,128)} %param.15) | copy-start | bytes 393220
  6.5 32.6 %copy-start.11 = (s32[4,1024]{1,0:T(4,128)S(1)}, s32[4,1024]{1,0:T(4,128)}, u32[]{:S(2)}) copy-start(s32[4,1024]{1,0:T(4,128)} %param.13) | copy-start | bytes 49156
  6.5 82.4 %all-gather.2.cloned.1.call-start = ((), (), s32[]{:S(2)}) async-start(), calls=%async_computation | async-start | bytes 4325376 | tf_op jit(solution)/shard_map/all_gather | solution.py:109
  9.9 4.9 %collective-permute-start = (f32[4,32,256]{2,1,0:T(8,128)S(1)}, f32[4,32,256]{2,1,0:T(8,128)S(1)}, u32[]{:S(2)}, u32[]{:S(2)}) collective-permute-start(f32[4,32,256]{2,1,0:T(8,128)S(1)} %bitcast.71), channel_id=1, source_target_pairs={{0,32},{32,0},{64,96},{96,64},{128,160},{160,128},{192,224},{224,1... | collective-permute-start | bytes 393224 | tf_op jit(solution)/shard_map/ppermute | solution.py:88
  14.8 9.6 %collective-permute-start.1 = (f32[4,32,256]{2,1,0:T(8,128)S(1)}, f32[4,32,256]{2,1,0:T(8,128)S(1)}, u32[]{:S(2)}, u32[]{:S(2)}) collective-permute-start(f32[4,32,256]{2,1,0:T(8,128)S(1)} %broadcast_select_fusion), channel_id=1, source_target_pairs={{0,64},{32,96},{64,0},{96,32},{128,192},{160,224},{192,128},{224,1... | collective-permute-start | bytes 393224 | tf_op jit(solution)/shard_map/ppermute | solution.py:88
  24.5 9.4 %collective-permute-start.2 = (f32[4,32,256]{2,1,0:T(8,128)S(1)}, f32[4,32,256]{2,1,0:T(8,128)S(1)}, u32[]{:S(2)}, u32[]{:S(2)}) collective-permute-start(f32[4,32,256]{2,1,0:T(8,128)S(1)} %broadcast_select_fusion.1), channel_id=1, source_target_pairs={{0,128},{32,160},{64,192},{96,224},{128,0},{160,32},{192,64},{224,... | collective-permute-start | bytes 393224 | tf_op jit(solution)/shard_map/ppermute | solution.py:88
  39.1 10.3 %copy-start.9 = (s32[4,3]{1,0:T(4,128)S(1)}, s32[4,3]{1,0:T(4,128)}, u32[]{:S(2)}) copy-start(s32[4,3]{1,0:T(4,128)} %param.12) | copy-start | bytes 148
  135.0 9.3 %copy-start = (bf16[1024,256]{1,0:T(8,128)(2,1)S(1)}, bf16[1024,256]{1,0:T(8,128)(2,1)}, u32[]{:S(2)}) copy-start(bf16[1024,256]{1,0:T(8,128)(2,1)} %get-tuple-element.15) | copy-start | bytes 1572868
  135.0 9.3 %copy-start.1 = (bf16[1024,256]{1,0:T(8,128)(2,1)S(1)}, bf16[1024,256]{1,0:T(8,128)(2,1)}, u32[]{:S(2)}) copy-start(bf16[1024,256]{1,0:T(8,128)(2,1)} %get-tuple-element.16) | copy-start | bytes 1572868
  135.0 9.3 %copy-start.2 = (bf16[1024,256]{1,0:T(8,128)(2,1)S(1)}, bf16[1024,256]{1,0:T(8,128)(2,1)}, u32[]{:S(2)}) copy-start(bf16[1024,256]{1,0:T(8,128)(2,1)} %get-tuple-element.17) | copy-start | bytes 1572868
  135.0 9.3 %copy-start.3 = (bf16[1024,256]{1,0:T(8,128)(2,1)S(1)}, bf16[1024,256]{1,0:T(8,128)(2,1)}, u32[]{:S(2)}) copy-start(bf16[1024,256]{1,0:T(8,128)(2,1)} %get-tuple-element.18) | copy-start | bytes 1572868
  135.0 9.3 %copy-start.4 = (bf16[1024,256]{1,0:T(8,128)(2,1)S(1)}, bf16[1024,256]{1,0:T(8,128)(2,1)}, u32[]{:S(2)}) copy-start(bf16[1024,256]{1,0:T(8,128)(2,1)} %get-tuple-element.13) | copy-start | bytes 1572868
  135.0 9.3 %copy-start.5 = (bf16[1024,256]{1,0:T(8,128)(2,1)S(1)}, bf16[1024,256]{1,0:T(8,128)(2,1)}, u32[]{:S(2)}) copy-start(bf16[1024,256]{1,0:T(8,128)(2,1)} %get-tuple-element.14) | copy-start | bytes 1572868
Sparse Core Ops, SparseCore 0:
  34.8 54.0 all-gather.1

commit v2 on v1

--- a/solution.py
+++ b/solution.py
@@ -21,12 +21,22 @@
 
 
 def adjust_kernel(prior_ref, values_ref, errors_ref, scaled_ref, incr_ref):
-    scaled, obs_incr = adjust(prior_ref[...], values_ref[...][:, 0], errors_ref[...][:, 0])
-    scaled_ref[...] = scaled
-    incr_ref[...] = obs_incr
+    prior_ens = prior_ref[...]
+    members = prior_ens.shape[1]
+    values = values_ref[...]
+    errors = errors_ref[...]
+    prior_mean = jnp.mean(prior_ens, axis=1, keepdims=True)
+    anomalies = prior_ens - prior_mean
+    variance = jnp.sum(anomalies * anomalies, axis=1, keepdims=True) / (members - 1) + 1e-05
+    post_var = variance * errors / (variance + errors)
+    mean_shift = post_var * (prior_mean / variance + values / errors) - prior_mean
+    shrink = jnp.sqrt(errors / (variance + errors))
+    incr_ref[...] = (mean_shift + (shrink - 1.0) * anomalies).astype(jnp.bfloat16)
+    inverse = 1.0 / ((members - 1) * variance)
+    scaled_ref[...] = (anomalies * inverse).astype(jnp.bfloat16)
 
 
-def adjust_rows(prior, values, errors, block=256):
+def adjust_rows(prior, values, errors, block=512):
     rows, members = prior.shape
     row_spec = pl.BlockSpec((block, members), lambda i: (i, 0))
     col_spec = pl.BlockSpec((block, 1), lambda i: (i, 0))
@@ -55,10 +65,7 @@
     for batch_idx in range(scaled_ref.shape[0]):
         centre = jnp.mean(current, axis=1, keepdims=True)
         state_anom = (current - centre).astype(jnp.bfloat16)
-        linked = lax.dot_general(
-            state_anom, scaled_ref[batch_idx], (((1,), (1,)), ((), ())),
-            preferred_element_type=jnp.float32,
-        )
+        linked = jnp.dot(state_anom, scaled_ref[batch_idx], preferred_element_type=jnp.float32)
         coupling = (linked * weights_ref[0, batch_idx]).astype(jnp.bfloat16)
         current = current + jnp.dot(coupling, incr_ref[batch_idx], preferred_element_type=jnp.float32)
     out_ref[...] = current
@@ -67,13 +74,14 @@
 def update_rows(block_x, scaled, obs_incr, weights, group_rows, block=256):
     rows, members = block_x.shape
     row_spec = pl.BlockSpec((block, members), lambda i: (i, 0))
-    full_spec = pl.BlockSpec(scaled.shape, lambda i: (0, 0, 0))
+    scaled_spec = pl.BlockSpec(scaled.shape, lambda i: (0, 0, 0))
+    incr_spec = pl.BlockSpec(obs_incr.shape, lambda i: (0, 0, 0))
     per_group = group_rows // block
     weight_spec = pl.BlockSpec((1,) + weights.shape[1:], lambda i: (i // per_group, 0, 0, 0))
     return pl.pallas_call(
         update_kernel,
         grid=(rows // block,),
-        in_specs=[row_spec, full_spec, full_spec, weight_spec],
+        in_specs=[row_spec, scaled_spec, incr_spec, weight_spec],
         out_specs=row_spec,
         out_shape=jax.ShapeDtypeStruct(block_x.shape, block_x.dtype),
     )(block_x, scaled, obs_incr, weights)
@@ -139,11 +147,11 @@
             ]
         )
         moved = update_rows(
-            block_x, scaled[None], obs_incr[None], weights[:, None, None, :], obs_count
+            block_x, scaled.T[None], obs_incr[None], weights[:, None, None, :], obs_count
         ).reshape(len(later), obs_count, members)
         for position, k in enumerate(later):
             pending[k] = moved[position]
-    scaled_all = jnp.stack(scaled_list)
+    scaled_all = jnp.swapaxes(jnp.stack(scaled_list), 1, 2)
     incr_all = jnp.stack(incr_list)
 
     main_weights = jnp.where(reads[:, region_idx, None], slot_taper[:, region_idx], 0.0)

time: 176 us -> 180 us (1.023)
  local copies, waits for them, and re-layouts: 25.6 us -> 32.9 us
  Pallas kernels: 62.2 us -> 57.3 us
    pallas_call x0 -> x4, local copies, waits for them, and re-layouts: none -> 7.36 us  [adjust_rows(): pl.pallas_call(adjust_kernel, grid=(rows // block,), in_specs=[row_spec,...]
    pallas_call x4, Pallas kernels: 16.7 us -> 11.9 us  [adjust_rows(): pl.pallas_call(adjust_kernel, grid=(rows // block,), in_specs=[row_spec,...]
where the time goes in v2:
time: 180 us; the launch traced here: 179 us
  Pallas kernels  57.3 us (32%)
  waiting for transfers between devices  34 us (19%)
  local copies, waits for them, and re-layouts  32.9 us (18%)
  between operations  19.4 us (11%)
  other arithmetic  13.9 us (8%)
  starting transfers between devices  12.9 us (7%)
  matrix products  8.14 us (5%)
    pallas_call x4, Pallas kernels, update_rows(): pl.pallas_call(update_kernel, grid=(rows // block,), in_specs=[row_spec,...  45.5 us
    all_gather x1, waiting for transfers between devices, local(): raw = lax.all_gather(pieces, 'rows', axis=1, tiled=True)  23.7 us
    ppermute x3, starting transfers between devices, pick_owner(): partner = lax.ppermute(held, axis, [(i, i ^ step) for i in range(size)])  12.9 us
    pallas_call x4, Pallas kernels, adjust_rows(): pl.pallas_call(adjust_kernel, grid=(rows // block,), in_specs=[row_spec,...  11.9 us
    ppermute x3, waiting for transfers between devices, pick_owner(): partner = lax.ppermute(held, axis, [(i, i ^ step) for i in range(size)])  10.3 us
    dot_general x1, matrix products, local(): jnp.einsum('bsj,bjc->bsc', picks, table, precision=lax.Precision.HIGHEST)  8.14 us
    pallas_call x4, local copies, waits for them, and re-layouts, adjust_rows(): pl.pallas_call(adjust_kernel, grid=(rows // block,), in_specs=[row_spec,...  7.36 us
    slice x2, local copies, waits for them, and re-layouts, local(): pending[k] = moved[position]  5.25 us
  transfers between devices with their start and end apart: 4, of which 4 were waited for; matrix products, arithmetic and copies ran while one was open for 14% of the time, Pallas kernels for 0%

profile of v2, /device:TPU:1, one launch (start us, length us, event | category | flops | bytes accessed | tf_op | source)
XLA Modules:
  0.0 178.6 jit_solution(4612007556137161473)
XLA Ops:
  6.6 0.8 compare_select_fusion
  7.4 0.1 reshape.162
  7.5 2.3 %gather_fusion = f32[128,256]{1,0:T(8,128)S(1)} fusion(f32[2048,256]{1,0:T(8,128)} %x_ref.1, s32[1024]{0:T(1024)S(1)} %pad_clamp_fusion), kind=kCustom, calls=%fused_computation | custom fusion | bytes 262656 | tf_op jit(solution)/shard_map/gather | solution.py:115
  9.9 2.5 %collective-permute-start = (f32[4,32,256]{2,1,0:T(8,128)S(1)}, f32[4,32,256]{2,1,0:T(8,128)S(1)}, u32[]{:S(2)}, u32[]{:S(2)}) collective-permute-start(f32[4,32,256]{2,1,0:T(8,128)S(1)} %bitcast.81), channel_id=1, source_target_pairs={{0,32},{32,0},{64,96},{96,64},{128,160},{160,128},{192,224},{224,1... | collective-permute-start | bytes 393224 | tf_op jit(solution)/shard_map/ppermute | solution.py:96
  12.4 0.7 fusion.16
  13.1 1.7 collective-permute-done
  14.8 3.8 %collective-permute-start.1 = (f32[4,32,256]{2,1,0:T(8,128)S(1)}, f32[4,32,256]{2,1,0:T(8,128)S(1)}, u32[]{:S(2)}, u32[]{:S(2)}) collective-permute-start(f32[4,32,256]{2,1,0:T(8,128)S(1)} %broadcast_select_fusion), channel_id=1, source_target_pairs={{0,64},{32,96},{64,0},{96,32},{128,192},{160,224},{192,128},{224,1... | collective-permute-start | bytes 393224 | tf_op jit(solution)/shard_map/ppermute | solution.py:96
  18.7 5.8 %collective-permute-done.1 = f32[4,32,256]{2,1,0:T(8,128)S(1)} collective-permute-done((f32[4,32,256]{2,1,0:T(8,128)S(1)}, f32[4,32,256]{2,1,0:T(8,128)S(1)}, u32[]{:S(2)}, u32[]{:S(2)}) %collective-permute-start.1) | collective-permute-done | bytes 131104 | tf_op jit(solution)/shard_map/ppermute | solution.py:96
  24.5 6.5 %collective-permute-start.2 = (f32[4,32,256]{2,1,0:T(8,128)S(1)}, f32[4,32,256]{2,1,0:T(8,128)S(1)}, u32[]{:S(2)}, u32[]{:S(2)}) collective-permute-start(f32[4,32,256]{2,1,0:T(8,128)S(1)} %broadcast_select_fusion.1), channel_id=1, source_target_pairs={{0,128},{32,160},{64,192},{96,224},{128,0},{160,32},{192,64},{224,... | collective-permute-start | bytes 393224 | tf_op jit(solution)/shard_map/ppermute | solution.py:96
  31.0 2.9 %collective-permute-done.2 = f32[4,32,256]{2,1,0:T(8,128)S(1)} collective-permute-done((f32[4,32,256]{2,1,0:T(8,128)S(1)}, f32[4,32,256]{2,1,0:T(8,128)S(1)}, u32[]{:S(2)}, u32[]{:S(2)}) %collective-permute-start.2) | collective-permute-done | bytes 131104 | tf_op jit(solution)/shard_map/ppermute | solution.py:96
  33.9 0.7 broadcast_select_fusion.2
  34.7 0.7 fusion.23
  39.3 8.1 %fusion = f32[4,1024,10]{1,2,0:T(8,128)S(1)} fusion(s32[4,1024]{1,0:T(4,128)S(1)} %copy-done.11, f32[4,1024,8]{1,2,0:T(8,128)S(1)} %bitcast.84, f32[4,1024,1]{1,2,0:T(1,128)S(1)} %broadcast_in_dim.87, f32[4,1024,1]{1,2,0:T(1,128)S(1)} %broadcast_in_dim.86), kind=kOutput, calls=%fused_computation.2 | convolution fusion | flops 507592704 | bytes 344064 | tf_op jit(solution)/shard_map/bsj,bjc->bsc/dot_general | solution.py:128
  47.6 1.0 copy.31.values_ref
  48.6 1.0 copy.32.errors_ref
  49.6 0.1 copy.35
  51.8 0.7 constant_dynamic-slice_fusion.7
  52.5 4.4 %fusion.13 = (f32[1,1,1,1024]{3,2,1,0:T(1,128)}, f32[1,1024]{1,0:T(1,128)S(1)}, f32[1,1024]{1,0:T(1,128)S(1)}, f32[1,1024]{1,0:T(1,128)S(1)}, f32[1,1024]{1,0:T(1,128)S(1)}, /*index=5*/f32[1,1024]{1,0:T(1,128)S(1)}) fusion(pred[]{:T(512)} %bitcast.37, f32[4,1024,8]{1,2,0:T(8,128)S(1)} %slice.119, s32[]{:T(128)S(6)} %select_n.216, pred[]{:T(512)} %bitcast.29, ...), kind=kLoop, calls=%fused_computation.36 | loop fusion | flops 6144 | bytes 49170 | tf_op jit(solution)/shard_map/jit(_where)/select_n | solution.py:145
  56.9 0.6 broadcast_in_dim.91.weights_ref
  57.5 1.0 copy.36.values_ref
  58.6 1.1 copy.37.errors_ref
  59.6 0.6 broadcast_in_dim.94.weights_ref
  60.3 1.1 copy.40.values_ref
  61.3 1.0 copy.41.errors_ref
  62.4 1.0 copy.44.values_ref
  63.4 1.0 copy.45.errors_ref
  64.4 0.2 fusion.15
  64.6 0.7 broadcast_select_fusion.3.weights_ref
  65.3 23.7 %all-gather.2.cloned.1.call-done = f32[4,1024,256]{2,1,0:T(8,128)} async-done(((f32[4,32,256]{2,1,0:T(8,128)}), f32[4,1024,256]{2,1,0:T(8,128)}) %all-gather.2.cloned.1.call-update) | async-done | bytes 4194320 | tf_op jit(solution)/shard_map/all_gather | solution.py:117
  88.9 3.6 %slice_bitcast_fusion.3 = (f32[1024,256]{1,0:T(8,128)}, f32[1024,256]{1,0:T(8,128)S(1)}, f32[1024,256]{1,0:T(8,128)S(1)}, f32[1024,256]{1,0:T(8,128)S(1)}) fusion(f32[4,1024,256]{2,1,0:T(8,128)} %all-gather.2.cloned.1.call-done), kind=kLoop, calls=%fused_computation.10 | loop fusion | bytes 8388608 | tf_op jit(solution)/shard_map/squeeze | solution.py:133
  92.5 3.0 %shard_map.82 = (bf16[1024,256]{1,0:T(8,128)(2,1)}, bf16[1024,256]{1,0:T(8,128)(2,1)}) custom-call(f32[1024,256]{1,0:T(8,128)} %get-tuple-element.21.prior_ref, f32[1024,1]{1,0:T(8,128)} %copy.31.values_ref, f32[1024,1]{1,0:T(8,128)} %copy.32.errors_ref), custom_call_target="tpu_custom_call" | custom-call | tf_op jit(solution)/shard_map/pallas_call | solution.py:44
  95.5 2.0 %copy.33 = bf16[1024,256]{0,1:T(8,128)(2,1)} copy(bf16[1024,256]{1,0:T(8,128)(2,1)} %get-tuple-element.13) | data formatting | bytes 1048576 | tf_op jit(solution)/shard_map/pallas_call | solution.py:44
  97.6 1.9 %pad_maximum_fusion.x_ref = f32[3072,256]{1,0:T(8,128)} fusion(f32[1024,256]{1,0:T(8,128)S(1)} %get-tuple-element.22, f32[1024,256]{1,0:T(8,128)S(1)} %get-tuple-element.23, f32[1024,256]{1,0:T(8,128)S(1)} %get-tuple-element.24), kind=kLoop, calls=%fused_computation.4 | loop fusion | flops 1572864 | bytes 6291456 | tf_op jit(solution)/shard_map/concatenate | solution.py:142
  99.4 11.6 %shard_map.83 = f32[3072,256]{1,0:T(8,128)} custom-call(f32[3072,256]{1,0:T(8,128)} %pad_maximum_fusion.x_ref, bf16[1,256,1024]{2,1,0:T(8,128)(2,1)} %bitcast.72, bf16[1,1024,256]{2,1,0:T(8,128)(2,1)} %bitcast.79, f32[3,1,1,1024]{3,2,1,0:T(1,128)} %broadcast_in_dim.91.weights_ref), custom_call_target="tpu_custom_call" | custom-call | tf_op jit(solution)/shard_map/pallas_call | solution.py:81
  111.0 2.3 %slice.120.prior_ref = f32[1024,256]{1,0:T(8,128)} slice(f32[3072,256]{1,0:T(8,128)} %shard_map.83), slice={[0:1024], [0:256]} | slice | bytes 2097152 | tf_op jit(solution)/shard_map/slice | solution.py:153
  113.3 3.0 %concatenate.12.x_ref = f32[2048,256]{1,0:T(8,128)} slice(f32[3072,256]{1,0:T(8,128)} %shard_map.83), slice={[1024:3072], [0:256]} | slice | bytes 4194304 | tf_op jit(solution)/shard_map/concatenate | solution.py:142
  116.3 3.0 %shard_map.84 = (bf16[1024,256]{1,0:T(8,128)(2,1)}, bf16[1024,256]{1,0:T(8,128)(2,1)}) custom-call(f32[1024,256]{1,0:T(8,128)} %slice.120.prior_ref, f32[1024,1]{1,0:T(8,128)} %copy.36.values_ref, f32[1024,1]{1,0:T(8,128)} %copy.37.errors_ref), custom_call_target="tpu_custom_call" | custom-call | tf_op jit(solution)/shard_map/pallas_call | solution.py:44
  119.3 2.0 %copy.38 = bf16[1024,256]{0,1:T(8,128)(2,1)} copy(bf16[1024,256]{1,0:T(8,128)(2,1)} %get-tuple-element.15) | data formatting | bytes 1048576 | tf_op jit(solution)/shard_map/pallas_call | solution.py:44
  121.3 8.2 %shard_map.85 = f32[2048,256]{1,0:T(8,128)} custom-call(f32[2048,256]{1,0:T(8,128)} %concatenate.12.x_ref, bf16[1,256,1024]{2,1,0:T(8,128)(2,1)} %bitcast.68, bf16[1,1024,256]{2,1,0:T(8,128)(2,1)} %bitcast.74, f32[2,1,1,1024]{3,2,1,0:T(1,128)} %broadcast_in_dim.94.weights_ref), custom_call_target="tpu_custom_call" | custom-call | tf_op jit(solution)/shard_map/pallas_call | solution.py:81
  129.6 3.0 %fusion.22 = (f32[1024,256]{1,0:T(8,128)}, f32[1024,256]{1,0:T(8,128)}) fusion(f32[2048,256]{1,0:T(8,128)} %shard_map.85), kind=kLoop, calls=%fused_computation.78 | loop fusion | bytes 4194304 | tf_op jit(solution)/shard_map/slice | solution.py:153
  132.6 3.0 %shard_map.86 = (bf16[1024,256]{1,0:T(8,128)(2,1)}, bf16[1024,256]{1,0:T(8,128)(2,1)}) custom-call(f32[1024,256]{1,0:T(8,128)} %get-tuple-element.25.prior_ref, f32[1024,1]{1,0:T(8,128)} %copy.40.values_ref, f32[1024,1]{1,0:T(8,128)} %copy.41.errors_ref), custom_call_target="tpu_custom_call" | custom-call | tf_op jit(solution)/shard_map/pallas_call | solution.py:44
  135.5 2.0 %copy.42 = bf16[1024,256]{0,1:T(8,128)(2,1)} copy(bf16[1024,256]{1,0:T(8,128)(2,1)} %get-tuple-element.17) | data formatting | bytes 1048576 | tf_op jit(solution)/shard_map/pallas_call | solution.py:44
  137.6 5.0 %shard_map.87.prior_ref = f32[1024,256]{1,0:T(8,128)} custom-call(f32[1024,256]{1,0:T(8,128)} %get-tuple-element.26.x_ref, bf16[1,256,1024]{2,1,0:T(8,128)(2,1)} %bitcast.70, bf16[1,1024,256]{2,1,0:T(8,128)(2,1)} %bitcast.77, f32[1,1,1,1024]{3,2,1,0:T(1,128)} %get-tuple-element.35.weights_ref), custom_call_target="tpu_custom_call" | custom-call | tf_op jit(solution)/shard_map/pallas_call | solution.py:81
  142.6 3.0 %shard_map.88 = (bf16[1024,256]{1,0:T(8,128)(2,1)}, bf16[1024,256]{1,0:T(8,128)(2,1)}) custom-call(f32[1024,256]{1,0:T(8,128)} %shard_map.87.prior_ref, f32[1024,1]{1,0:T(8,128)} %copy.44.values_ref, f32[1024,1]{1,0:T(8,128)} %copy.45.errors_ref), custom_call_target="tpu_custom_call" | custom-call | tf_op jit(solution)/shard_map/pallas_call | solution.py:44
  145.6 2.7 %pad_maximum_fusion.1.incr_ref = bf16[4,1024,256]{2,1,0:T(8,128)(2,1)} fusion(bf16[1,1024,256]{2,1,0:T(8,128)(2,1)} %bitcast.83, bf16[1,1024,256]{2,1,0:T(8,128)(2,1)S(1)} %bitcast.78, bf16[1,1024,256]{2,1,0:T(8,128)(2,1)S(1)} %bitcast.75, bf16[1,1024,256]{2,1,0:T(8,128)(2,1)S(1)} %bitcast.80), kind=kLoop, calls=%fused_computation.6 | loop fusion | flops 3145728 | bytes 4194304 | tf_op jit(solution)/shard_map/stack | solution.py:155
  148.3 1.2 copy.46
  149.6 1.6 maximum_bitcast_fusion.scaled_ref
  151.2 20.6 %shard_map.89 = f32[2048,256]{1,0:T(8,128)} custom-call(f32[2048,256]{1,0:T(8,128)} %x_ref.1, bf16[4,256,1024]{2,1,0:T(8,128)(2,1)} %maximum_bitcast_fusion.scaled_ref, bf16[4,1024,256]{2,1,0:T(8,128)(2,1)} %pad_maximum_fusion.1.incr_ref, f32[1,4,1,1024]{3,2,1,0:T(1,128)} %broadcast_select_fusion.3.weights_ref), custom_call_target="tpu_custom_call" | custom-call | tf_op jit(solution)/shard_map/pallas_call | solution.py:81
  (37 shorter events, 0.5 us)
Async XLA Ops:
  6.5 28.2 %copy-start.8 = (s32[4]{0:T(128)S(1)}, s32[4]{0:T(128)}, u32[]{:S(2)}) copy-start(s32[4]{0:T(128)} %param.11) | copy-start | bytes 52
  6.5 32.7 %copy-start.6 = (f32[4,1024]{1,0:T(4,128)S(1)}, f32[4,1024]{1,0:T(4,128)}, u32[]{:S(2)}) copy-start(f32[4,1024]{1,0:T(4,128)} %param.9) | copy-start | bytes 49156
  6.5 32.7 %copy-start.7 = (f32[4,1024]{1,0:T(4,128)S(1)}, f32[4,1024]{1,0:T(4,128)}, u32[]{:S(2)}) copy-start(f32[4,1024]{1,0:T(4,128)} %param.10) | copy-start | bytes 49156
  6.5 32.8 %copy-start.10 = (f32[4,8,1024]{2,1,0:T(8,128)S(1)}, f32[4,8,1024]{2,1,0:T(8,128)}, u32[]{:S(2)}) copy-start(f32[4,8,1024]{2,1,0:T(8,128)} %param.15) | copy-start | bytes 393220
  6.5 32.8 %copy-start.11 = (s32[4,1024]{1,0:T(4,128)S(1)}, s32[4,1024]{1,0:T(4,128)}, u32[]{:S(2)}) copy-start(s32[4,1024]{1,0:T(4,128)} %param.13) | copy-start | bytes 49156
  6.5 82.4 %all-gather.2.cloned.1.call-start = ((), (), s32[]{:S(2)}) async-start(), calls=%async_computation | async-start | bytes 4325376 | tf_op jit(solution)/shard_map/all_gather | solution.py:117
  9.9 4.9 %collective-permute-start = (f32[4,32,256]{2,1,0:T(8,128)S(1)}, f32[4,32,256]{2,1,0:T(8,128)S(1)}, u32[]{:S(2)}, u32[]{:S(2)}) collective-permute-start(f32[4,32,256]{2,1,0:T(8,128)S(1)} %bitcast.81), channel_id=1, source_target_pairs={{0,32},{32,0},{64,96},{96,64},{128,160},{160,128},{192,224},{224,1... | collective-permute-start | bytes 393224 | tf_op jit(solution)/shard_map/ppermute | solution.py:96
  14.8 9.6 %collective-permute-start.1 = (f32[4,32,256]{2,1,0:T(8,128)S(1)}, f32[4,32,256]{2,1,0:T(8,128)S(1)}, u32[]{:S(2)}, u32[]{:S(2)}) collective-permute-start(f32[4,32,256]{2,1,0:T(8,128)S(1)} %broadcast_select_fusion), channel_id=1, source_target_pairs={{0,64},{32,96},{64,0},{96,32},{128,192},{160,224},{192,128},{224,1... | collective-permute-start | bytes 393224 | tf_op jit(solution)/shard_map/ppermute | solution.py:96
  24.5 9.4 %collective-permute-start.2 = (f32[4,32,256]{2,1,0:T(8,128)S(1)}, f32[4,32,256]{2,1,0:T(8,128)S(1)}, u32[]{:S(2)}, u32[]{:S(2)}) collective-permute-start(f32[4,32,256]{2,1,0:T(8,128)S(1)} %broadcast_select_fusion.1), channel_id=1, source_target_pairs={{0,128},{32,160},{64,192},{96,224},{128,0},{160,32},{192,64},{224,... | collective-permute-start | bytes 393224 | tf_op jit(solution)/shard_map/ppermute | solution.py:96
  39.3 10.3 %copy-start.9 = (s32[4,3]{1,0:T(4,128)S(1)}, s32[4,3]{1,0:T(4,128)}, u32[]{:S(2)}) copy-start(s32[4,3]{1,0:T(4,128)} %param.12) | copy-start | bytes 148
  137.5 8.0 %copy-start.3 = (bf16[1024,256]{1,0:T(8,128)(2,1)S(1)}, bf16[1024,256]{1,0:T(8,128)(2,1)}, u32[]{:S(2)}) copy-start(bf16[1024,256]{1,0:T(8,128)(2,1)} %get-tuple-element.16) | copy-start | bytes 1572868
  137.5 8.0 %copy-start.4 = (bf16[1024,256]{1,0:T(8,128)(2,1)S(1)}, bf16[1024,256]{1,0:T(8,128)(2,1)}, u32[]{:S(2)}) copy-start(bf16[1024,256]{1,0:T(8,128)(2,1)} %get-tuple-element.18) | copy-start | bytes 1572868
  137.5 8.0 %copy-start.5 = (bf16[1024,256]{1,0:T(8,128)(2,1)S(1)}, bf16[1024,256]{1,0:T(8,128)(2,1)}, u32[]{:S(2)}) copy-start(bf16[1024,256]{1,0:T(8,128)(2,1)} %get-tuple-element.14) | copy-start | bytes 1572868
  145.5 4.0 %copy-start = (bf16[1024,256]{0,1:T(8,128)(2,1)S(1)}, bf16[1024,256]{0,1:T(8,128)(2,1)}, u32[]{:S(2)}) copy-start(bf16[1024,256]{0,1:T(8,128)(2,1)} %copy.38) | copy-start | bytes 1572868
  145.5 4.0 %copy-start.1 = (bf16[1024,256]{0,1:T(8,128)(2,1)S(1)}, bf16[1024,256]{0,1:T(8,128)(2,1)}, u32[]{:S(2)}) copy-start(bf16[1024,256]{0,1:T(8,128)(2,1)} %copy.42) | copy-start | bytes 1572868
  145.6 4.0 %copy-start.2 = (bf16[1024,256]{0,1:T(8,128)(2,1)S(1)}, bf16[1024,256]{0,1:T(8,128)(2,1)}, u32[]{:S(2)}) copy-start(bf16[1024,256]{0,1:T(8,128)(2,1)} %copy.33) | copy-start | bytes 1572868
Sparse Core Ops, SparseCore 0:
  34.8 54.0 all-gather.1
